TPU v7x, 256 devices: a whole 4x4x8 slice. The times are simulated.
256 devices in a mesh: seg: 8 (over y, core), sec: 32 (over x, z).
Axes of the slice: x: 4, y: 4, z: 8, core: 2. Of those that a mesh axis runs over, the one named last changes fastest.
Arguments:
- psi_init: float32 [8, 32, 256, 256], P('seg', 'sec'), may hold values from -6 to 6
- boundary_env: float32 [32, 18, 256, 256], P('sec')
- right_env: float32 [8, 32, 18, 256, 256], P('seg', 'sec')
- transfer_blocks: float32 [8, 32, 256, 256], P('seg', 'sec')
- transfer_mix: float32 [8, 18, 18], P('seg')
- hop_left: float32 [8, 32, 256, 256], P('seg', 'sec'), may hold values from -0.75 to 0.75
- hop_right: float32 [8, 32, 256, 256], P('seg', 'sec'), may hold values from -0.75 to 0.75
- block_sizes: int32 [8, 2, 32], P('seg'), may hold values from 64 to 256, as said below
- sources: int32 [8, 32], P('seg'), may hold values from 0 to 31, each once within a row
Outputs:
- state: float32 [8, 32, 256, 256], P('seg', 'sec')
Inputs may be any that keep to these rules, and one draw needn't show every extreme that they name: `sources`: each block number appears once in a segment's list. `block_sizes`: each segment has a block with 256 live rows and one with 256 live columns.
All inputs are finite; a program needn't handle non-finite values.
Results may differ from a plain program's by a relative error of at most 0.0003.
Values sent between devices are 32-bit elements; how exact they have to be, the bound alone decides.
No kernel may reach another device: no remote copies, remote signals or barrier semaphores. Data moves between devices by JAX's collectives and lax.ppermute only.
A program may use at most 128 MiB of HBM per device.

v0:
```python
import jax
import jax.numpy as jnp
from jax import lax
from jax.sharding import PartitionSpec as P

DAV = 2
HIGH = lax.Precision.HIGHEST
EPSILON = 1e-06


def passed_along(value, axis, steps):
    count = lax.axis_size(axis)
    initial, last = (max(0, -steps), min(count, count - steps))
    return lax.ppermute(value, axis, [(source, source + steps) for source in range(initial, last)])


def product(left, right):
    return jnp.matmul(left, right, precision=HIGH)


def combine(earlier, later):
    return (product(earlier[0], later[0]), product(earlier[1], later[1]))


def norm_total(vector):
    return lax.psum(jnp.sum(vector * vector), "sec")


def per_device(
    psi_init,
    boundary_env,
    right_env,
    transfer_blocks,
    transfer_mix,
    hop_left,
    hop_right,
    block_sizes,
    sources,
):
    initial = psi_init[0]
    right_side = right_env[0]
    own_blocks = transfer_blocks[0]
    own_mix = transfer_mix[0]
    left_hop = hop_left[0]
    right_hop = hop_right[0]
    all_sizes = block_sizes[0]
    all_sources = sources[0]
    local_blocks = initial.shape[0]
    block_width = initial.shape[1]
    channels = own_mix.shape[0]
    sector_count = lax.axis_size("sec")
    first_block = lax.axis_index("sec") * local_blocks
    eye_mix = jnp.eye(channels, dtype=jnp.float32)
    eye_blocks = jnp.broadcast_to(jnp.eye(block_width, dtype=jnp.float32), own_blocks.shape)
    prefix_mix, prefix_blocks = (eye_mix, eye_blocks)
    leading = lax.axis_index("seg") == 0
    for hop_index in range(lax.axis_size("seg") - 1):
        carry_mix, carry_blocks = combine((prefix_mix, prefix_blocks), (own_mix, own_blocks))
        got_mix, got_blocks = passed_along((carry_mix, carry_blocks), "seg", 1)
        prefix_mix = jnp.where(leading, eye_mix, got_mix)
        prefix_blocks = jnp.where(leading, eye_blocks, got_blocks)
    turned = product(
        product(jnp.swapaxes(prefix_blocks, 1, 2)[:, None], boundary_env), prefix_blocks[:, None]
    )
    left_env = jnp.einsum("vw,bvij->bwij", prefix_mix, turned, precision=HIGH)
    live_sizes = lax.dynamic_slice_in_dim(all_sizes, first_block, local_blocks, 1)
    wanted = lax.dynamic_slice_in_dim(all_sources, first_block, local_blocks, 0)
    places = lax.broadcasted_iota(jnp.int32, (1, block_width), 1)
    row_live = (places < live_sizes[0][:, None]).astype(jnp.float32)
    col_live = (places < live_sizes[1][:, None]).astype(jnp.float32)
    masking = row_live[:, :, None] * col_live[:, None, :]
    diagonal = jnp.einsum(
        "bwi,bwj->bij",
        jnp.diagonal(left_env, axis1=2, axis2=3),
        jnp.diagonal(right_side, axis1=2, axis2=3),
        precision=HIGH,
    )
    vector = masking * initial
    vector = vector / jnp.sqrt(norm_total(vector) + EPSILON)
    for turn_index in range(DAV):
        local_part = jnp.sum(product(product(left_env, vector[:, None]), right_side), axis=1)
        moving = product(vector, right_hop)
        shard_piece = lax.all_gather(moving, "sec", axis=0, tiled=True)
        global_ids = lax.broadcasted_iota(jnp.int32, (1, shard_piece.shape[0]), 1)
        chooser = (wanted[:, None] == global_ids).astype(jnp.float32)
        regrouped = jnp.zeros_like(moving) + jnp.einsum(
            "ji,ipc->jpc", chooser, shard_piece, precision=HIGH
        )
        image_vec = masking * (local_part + product(left_hop, regrouped))
        rayleigh = lax.psum(jnp.sum(vector * image_vec), "sec")
        residue = image_vec - rayleigh * vector
        shifted = diagonal - rayleigh
        update = vector - residue * shifted / (shifted * shifted + 1.0)
        vector = update / jnp.sqrt(norm_total(update) + EPSILON)
    cells = float(local_blocks * sector_count * block_width * block_width)
    return (vector * jnp.sqrt(jnp.float32(cells)))[None]


def solution(mesh):
    return jax.shard_map(
        per_device,
        mesh=mesh,
        in_specs=(
            P("seg", "sec", None, None),
            P("sec", None, None, None),
            P("seg", "sec", None, None, None),
            P("seg", "sec", None, None),
            P("seg", None, None),
            P("seg", "sec", None, None),
            P("seg", "sec", None, None),
            P("seg", None, None),
            P("seg", None),
        ),
        out_specs=P("seg", "sec", None, None),
        check_vma=False,
    )
```

profile of v0, /device:TPU:8, one launch (start us, length us, event | category | flops | bytes accessed | tf_op | source)
XLA Modules:
  0.0 646.8 jit_solution(14586238692061087781)
XLA Ops:
  10.8 78.3 %psum.35 = f32[]{:T(128)} all-reduce(f32[]{:T(128)} %fusion.65), channel_id=1, replica_groups=mesh['seg'=8,'sec'=32] {'sec'}, use_global_device_ids=true, to_apply=%region_1.2 | all-reduce | flops 1 | bytes 8 | tf_op jit(solution)/shard_map/psum | solution.py:26
  94.2 5.8 collective-permute-done
  102.3 5.8 collective-permute-done.1
  110.4 5.8 collective-permute-done.2
  119.3 3.6 collective-permute-start.7
  127.6 3.6 collective-permute-start.4
  133.3 3.1 collective-permute-done.9
  138.8 3.3 collective-permute-start.5
  153.0 18.1 %copy.26 = f32[1,1,18,256,256]{2,4,3,1,0:T(8,128)} copy(f32[1,1,18,256,256]{4,3,2,1,0:T(8,128)} %param.11) | data formatting | bytes 9437184 | tf_op args[2]
  175.8 6.1 fusion.12
  181.9 4.0 fusion.10
  186.0 10.1 %fusion.18 = f32[18,256,256]{2,0,1:T(8,128)} fusion(f32[18,256,256]{2,1,0:T(8,128)S(1)} %fusion.10, f32[18,18]{1,0:T(8,128)S(1)} %collective-permute-done.13, pred[]{:T(512)S(6)} %eq.62), kind=kOutput, calls=%fused_computation.20 | convolution fusion | flops 254804944 | bytes 9438481 | tf_op jit(solution)/shard_map/vw,bvij->bwij/dot_general | solution.py:65
  196.1 17.6 %copy.29 = f32[18,256,256]{0,2,1:T(8,128)} copy(f32[18,256,256]{2,0,1:T(8,128)} %fusion.18) | data formatting | bytes 9437184 | tf_op jit(solution)/shard_map/squeeze | solution.py:18
  216.0 7.9 %fusion.16 = f32[18,256,256]{2,1,0:T(8,128)S(1)} fusion(f32[18,256,256]{2,0,1:T(8,128)} %fusion.18, f32[1,1,256,256]{3,2,1,0:T(8,128)S(1)} %copy-done.2, f32[]{:T(128)S(6)} %sqrt.9, f32[256]{0:T(256)S(1)} %get-tuple-element.16, f32[256]{0:T(256)S(1)} %get-tuple-element.17), kind=kOutput, calls=%fused_computation.18 | convolution fusion | flops 3624075264 | bytes 9701380 | tf_op jit(solution)/shard_map/dot_general | solution.py:18
  223.9 9.9 %fusion.28 = f32[256,256]{1,0:T(8,128)S(1)} fusion(f32[18,256,256]{2,1,0:T(8,128)S(1)} %fusion.16, f32[1,1,18,256,256]{4,3,2,1,0:T(8,128)} %param.11), kind=kOutput, calls=%fused_computation.35 | convolution fusion | flops 3623878656 | bytes 9699328 | tf_op jit(solution)/shard_map/dot_general | solution.py:18
  233.9 11.0 %fusion.2 = f32[1,256,256]{2,0,1:T(1,128)S(1)} fusion(f32[32,256,256]{2,1,0:T(8,128)} %bitcast.185, s32[]{:T(128)} %bitcast.34), kind=kOutput, calls=%fused_computation.4 | convolution fusion | flops 25165856 | bytes 8650756 | tf_op jit(solution)/shard_map/ji,ipc->jpc/dot_general | solution.py:86
  245.9 70.3 %psum.36 = f32[]{:T(128)} all-reduce(f32[]{:T(128)} %get-tuple-element.11), channel_id=1, replica_groups=mesh['seg'=8,'sec'=32] {'sec'}, use_global_device_ids=true, to_apply=%region_3.4 | all-reduce | flops 1 | bytes 8 | tf_op jit(solution)/shard_map/psum | solution.py:90
  317.9 72.1 %psum.37 = f32[]{:T(128)} all-reduce(f32[]{:T(128)} %get-tuple-element.7), channel_id=1, replica_groups=mesh['seg'=8,'sec'=32] {'sec'}, use_global_device_ids=true, to_apply=%region_5.6 | all-reduce | flops 1 | bytes 8 | tf_op jit(solution)/shard_map/psum | solution.py:26
  391.9 7.8 %fusion.14 = f32[18,256,256]{2,1,0:T(8,128)S(1)} fusion(f32[18,256,256]{2,0,1:T(8,128)} %fusion.18, f32[256,256]{1,0:T(8,128)S(1)} %get-tuple-element.8, f32[]{:T(128)S(6)} %sqrt.10), kind=kOutput, calls=%fused_computation.16 | convolution fusion | flops 3623944192 | bytes 9699332 | tf_op jit(solution)/shard_map/dot_general | solution.py:18
  399.7 4.1 fusion.25
  403.8 78.8 %all-gather.7.cloned.1.call-done = f32[8192,256]{1,0:T(8,128)} async-done(((f32[256,256]{1,0:T(8,128)}), f32[8192,256]{1,0:T(8,128)}) %all-gather.7.cloned.1.call-update) | async-done | bytes 8388624 | tf_op jit(solution)/shard_map/all_gather | solution.py:83
  482.6 11.0 %fusion = f32[1,256,256]{2,0,1:T(1,128)S(1)} fusion(f32[32,256,256]{2,1,0:T(8,128)} %bitcast.186, s32[]{:T(128)} %bitcast.34), kind=kOutput, calls=%fused_computation.2 | convolution fusion | flops 25165856 | bytes 8650756 | tf_op jit(solution)/shard_map/ji,ipc->jpc/dot_general | solution.py:86
  494.7 71.9 %psum.38 = f32[]{:T(128)} all-reduce(f32[]{:T(128)} %get-tuple-element.14), channel_id=1, replica_groups=mesh['seg'=8,'sec'=32] {'sec'}, use_global_device_ids=true, to_apply=%region_7.8 | all-reduce | flops 1 | bytes 8 | tf_op jit(solution)/shard_map/psum | solution.py:90
  567.9 70.5 %psum.39 = f32[]{:T(128)} all-reduce(f32[]{:T(128)} %get-tuple-element.5), channel_id=1, replica_groups=mesh['seg'=8,'sec'=32] {'sec'}, use_global_device_ids=true, to_apply=%region_9.10 | all-reduce | flops 1 | bytes 8 | tf_op jit(solution)/shard_map/psum | solution.py:26
  (74 shorter events, 50.3 us)
Async XLA Ops:
  6.5 85.4 %copy-start = (f32[1,1,256,256]{3,2,1,0:T(8,128)S(1)}, f32[1,1,256,256]{3,2,1,0:T(8,128)}, u32[]{:S(2)}) copy-start(f32[1,1,256,256]{3,2,1,0:T(8,128)} %param.12) | copy-start | bytes 786436
  6.5 124.6 %copy-start.3 = (f32[1,18,18]{2,0,1:T(1,128)S(1)}, f32[1,18,18]{2,0,1:T(1,128)}, u32[]{:S(2)}) copy-start(f32[1,18,18]{2,0,1:T(1,128)} %param.13) | copy-start | bytes 3892
  6.5 145.9 %copy-start.6 = (s32[1,32]{1,0:T(1,128)S(1)}, s32[1,32]{1,0:T(1,128)}, u32[]{:S(2)}) copy-start(s32[1,32]{1,0:T(1,128)} %param.17) | copy-start | bytes 388
  6.5 227.3 %all-gather.5.cloned.1.call-start = ((), (), s32[]{:S(2)}) async-start(), calls=%async_computation | async-start | bytes 8650752 | tf_op jit(solution)/shard_map/all_gather | solution.py:83
  91.9 390.7 %all-gather.7.cloned.1.call-start = ((), (), s32[]{:S(2)}) async-start(), calls=%async_computation.1 | async-start | bytes 8650752 | tf_op jit(solution)/shard_map/all_gather | solution.py:83
  92.3 7.7 %collective-permute-start = (f32[1,256,256]{2,1,0:T(8,128)S(1)}, f32[1,256,256]{2,1,0:T(8,128)S(1)}, u32[]{:S(2)}, u32[]{:S(2)}) collective-permute-start(f32[1,256,256]{2,1,0:T(8,128)S(1)} %convolution_bitcast_fusion.8), channel_id=1, source_target_pairs={{0,32},{32,64},{64,96},{96,128},{128,160},{160,192},{192,224},{1,3... | collective-permute-start | bytes 786440 | tf_op jit(solution)/shard_map/ppermute | solution.py:14
  100.4 7.7 %collective-permute-start.1 = (f32[1,256,256]{2,1,0:T(8,128)S(1)}, f32[1,256,256]{2,1,0:T(8,128)S(1)}, u32[]{:S(2)}, u32[]{:S(2)}) collective-permute-start(f32[1,256,256]{2,1,0:T(8,128)S(1)} %convolution_bitcast_fusion.7), channel_id=1, source_target_pairs={{0,32},{32,64},{64,96},{96,128},{128,160},{160,192},{192,224},{1,3... | collective-permute-start | bytes 786440 | tf_op jit(solution)/shard_map/ppermute | solution.py:14
  108.5 7.7 %collective-permute-start.2 = (f32[1,256,256]{2,1,0:T(8,128)S(1)}, f32[1,256,256]{2,1,0:T(8,128)S(1)}, u32[]{:S(2)}, u32[]{:S(2)}) collective-permute-start(f32[1,256,256]{2,1,0:T(8,128)S(1)} %convolution_bitcast_fusion.6), channel_id=1, source_target_pairs={{0,32},{32,64},{64,96},{96,128},{128,160},{160,192},{192,224},{1,3... | collective-permute-start | bytes 786440 | tf_op jit(solution)/shard_map/ppermute | solution.py:14
  116.6 10.6 %collective-permute-start.3 = (f32[1,256,256]{2,1,0:T(8,128)S(1)}, f32[1,256,256]{2,1,0:T(8,128)S(1)}, u32[]{:S(2)}, u32[]{:S(2)}) collective-permute-start(f32[1,256,256]{2,1,0:T(8,128)S(1)} %convolution_bitcast_fusion.5), channel_id=1, source_target_pairs={{0,32},{32,64},{64,96},{96,128},{128,160},{160,192},{192,224},{1,3... | collective-permute-start | bytes 786440 | tf_op jit(solution)/shard_map/ppermute | solution.py:14
  119.3 5.1 collective-permute-start.7
  125.2 5.9 collective-permute-start.8
  127.6 10.9 %collective-permute-start.4 = (f32[1,256,256]{2,1,0:T(8,128)S(1)}, f32[1,256,256]{2,1,0:T(8,128)S(1)}, u32[]{:S(2)}, u32[]{:S(2)}) collective-permute-start(f32[1,256,256]{2,1,0:T(8,128)S(1)} %convolution_bitcast_fusion.4), channel_id=1, source_target_pairs={{0,32},{32,64},{64,96},{96,128},{128,160},{160,192},{192,224},{1,3... | collective-permute-start | bytes 786440 | tf_op jit(solution)/shard_map/ppermute | solution.py:14
  131.3 5.0 collective-permute-start.9
  136.5 5.6 collective-permute-start.10
  138.8 10.6 %collective-permute-start.5 = (f32[1,256,256]{2,1,0:T(8,128)S(1)}, f32[1,256,256]{2,1,0:T(8,128)S(1)}, u32[]{:S(2)}, u32[]{:S(2)}) collective-permute-start(f32[1,256,256]{2,1,0:T(8,128)S(1)} %convolution_bitcast_fusion.3), channel_id=1, source_target_pairs={{0,32},{32,64},{64,96},{96,128},{128,160},{160,192},{192,224},{1,3... | collective-permute-start | bytes 786440 | tf_op jit(solution)/shard_map/ppermute | solution.py:14
  142.3 5.0 collective-permute-start.11
  147.5 26.1 %collective-permute-start.12 = (f32[18,18]{1,0:T(8,128)S(1)}, f32[18,18]{1,0:T(8,128)S(1)}, u32[]{:S(2)}, u32[]{:S(2)}) collective-permute-start(f32[18,18]{1,0:T(8,128)S(1)} %fusion.80), channel_id=1, source_target_pairs={{0,32},{32,64},{64,96},{96,128},{128,160},{160,192},{192,224},{1,3... | collective-permute-start | bytes 3896 | tf_op jit(solution)/shard_map/ppermute | solution.py:14
  149.8 26.0 %collective-permute-start.6 = (f32[1,256,256]{2,1,0:T(8,128)S(1)}, f32[1,256,256]{2,1,0:T(8,128)S(1)}, u32[]{:S(2)}, u32[]{:S(2)}) collective-permute-start(f32[1,256,256]{2,1,0:T(8,128)S(1)} %convolution_bitcast_fusion.2), channel_id=1, source_target_pairs={{0,32},{32,64},{64,96},{96,128},{128,160},{160,192},{192,224},{1,3... | collective-permute-start | bytes 786440 | tf_op jit(solution)/shard_map/ppermute | solution.py:14
  173.7 12.3 %collective-permute-start.13 = (f32[18,18]{1,0:T(8,128)S(1)}, f32[18,18]{1,0:T(8,128)S(1)}, u32[]{:S(2)}, u32[]{:S(2)}) collective-permute-start(f32[18,18]{1,0:T(8,128)S(1)} %fusion.81), channel_id=1, source_target_pairs={{0,32},{32,64},{64,96},{96,128},{128,160},{160,192},{192,224},{1,3... | collective-permute-start | bytes 3896 | tf_op jit(solution)/shard_map/ppermute | solution.py:14
  196.1 20.0 %copy-start.2 = (f32[1,1,256,256]{3,2,1,0:T(8,128)S(1)}, f32[1,1,256,256]{3,2,1,0:T(8,128)}, u32[]{:S(2)}) copy-start(f32[1,1,256,256]{3,2,1,0:T(8,128)} %param.9) | copy-start | bytes 786436
  233.8 11.1 %copy-start.5 = (f32[1,1,256,256]{3,2,1,0:T(8,128)S(1)}, f32[1,1,256,256]{3,2,1,0:T(8,128)}, u32[]{:S(2)}) copy-start(f32[1,1,256,256]{3,2,1,0:T(8,128)} %param.14) | copy-start | bytes 786436
  233.9 156.9 %copy-start.4 = (f32[1,1,256,256]{3,2,1,0:T(8,128)S(1)}, f32[1,1,256,256]{3,2,1,0:T(8,128)}, u32[]{:S(2)}) copy-start(f32[1,1,256,256]{3,2,1,0:T(8,128)} %param.15) | copy-start | bytes 786436
  316.2 83.5 %slice-start = ((s8[4718592]{0:T(1024)(128)(4,1)}), s8[524288]{0:T(1024)(128)(4,1)S(1)}, s32[]{:S(2)}) async-start(s8[4718592]{0:T(1024)(128)(4,1)} %bitcast.182), calls=%async_computation.2 | async-start | bytes 1048576
  482.6 157.2 %copy-start.1 = (f32[1,1,256,256]{3,2,1,0:T(8,128)S(1)}, f32[1,1,256,256]{3,2,1,0:T(8,128)}, u32[]{:S(2)}) copy-start(f32[1,1,256,256]{3,2,1,0:T(8,128)} %param.12) | copy-start | bytes 786436
  (1 other events, 7.8 us)
Sparse Core Ops, SparseCore 0:
  92.1 91.5 all-gather.4
  392.0 90.6 all-gather.6
where the time goes:
time: 653 us; the launch traced here: 647 us
  blocking collectives  363 us (56%)
  waiting for transfers between devices  104 us (16%)
  matrix products  84 us (13%)
  local copies, waits for them, and re-layouts  42.3 us (6%)
  starting transfers between devices  32.6 us (5%)
  between operations  16.1 us (2%)
    psum x3, blocking collectives, norm_total(): return lax.psum(jnp.sum(vector * vector), 'sec')  221 us
    psum x2, blocking collectives, per_device(): rayleigh = lax.psum(jnp.sum(vector * image_vec), 'sec')  142 us
    all_gather x2, waiting for transfers between devices, per_device(): shard_piece = lax.all_gather(moving, 'sec', axis=0, tiled=True)  78.9 us
    dot_general x24, matrix products, product(): return jnp.matmul(left, right, precision=HIGH)  50 us
    ppermute x14, starting transfers between devices, passed_along(): lax.ppermute(value, axis, [(source, source + steps) for source in range(i...  32.5 us
    ppermute x14, waiting for transfers between devices, passed_along(): lax.ppermute(value, axis, [(source, source + steps) for source in range(i...  24.9 us
    dot_general x2, matrix products, per_device(): jnp.einsum('ji,ipc->jpc', chooser, shard_piece, precision=HIGH)  22 us
    unnamed x19, local copies, waits for them, and re-layouts  18.1 us
  transfers between devices with their start and end apart: 16, of which 7 were waited for; matrix products, arithmetic and copies ran while one was open for 15% of the time, Pallas kernels for 0%

commit v1 on v0

--- a/solution.py
+++ b/solution.py
@@ -80,7 +80,9 @@
     for turn_index in range(DAV):
         local_part = jnp.sum(product(product(left_env, vector[:, None]), right_side), axis=1)
         moving = product(vector, right_hop)
-        shard_piece = lax.all_gather(moving, "sec", axis=0, tiled=True)
+        shard_piece = jnp.concatenate(
+            lax.all_to_all(jnp.stack([moving] * lax.axis_size("sec")), "sec", 0, 0), axis=0
+        )
         global_ids = lax.broadcasted_iota(jnp.int32, (1, shard_piece.shape[0]), 1)
         chooser = (wanted[:, None] == global_ids).astype(jnp.float32)
         regrouped = jnp.zeros_like(moving) + jnp.einsum(

time: 653 us -> 747 us (1.14)
  waiting for transfers between devices: 104 us -> 184 us
  between operations: 16.1 us -> 3.03 us
  starting transfers between devices: 32.6 us -> 44.3 us
  local copies, waits for them, and re-layouts: 42.3 us -> 50.6 us
    all_to_all x0 -> x2, waiting for transfers between devices: none -> 158 us  [per_device(): lax.all_to_all(jnp.stack([moving] * lax.axis_size('sec')), 'sec', 0, 0)]
    all_gather x2 -> x0, waiting for transfers between devices: 78.9 us -> none  [per_device(): shard_piece = lax.all_gather(moving, 'sec', axis=0, tiled=True)]
    all_to_all x0 -> x2, starting transfers between devices: none -> 11.5 us  [per_device(): lax.all_to_all(jnp.stack([moving] * lax.axis_size('sec')), 'sec', 0, 0)]
    another operation x0 -> x2, local copies, waits for them, and re-layouts: none -> 8.31 us  [per_device(): jnp.stack([moving] * lax.axis_size('sec'))]
    unnamed x19 -> x15, local copies, waits for them, and re-layouts: 18.1 us -> 18.1 us
  transfers between devices with their start and end apart: 16 -> 16, of which waited for: 7 -> 8; matrix products, arithmetic and copies ran while one was open for 15% -> 13% of each run, Pallas kernels for 0% -> 0%
where the time goes in v1:
time: 747 us; the launch traced here: 740 us
  blocking collectives  366 us (49%)
  waiting for transfers between devices  184 us (25%)
  matrix products  86.6 us (12%)
  local copies, waits for them, and re-layouts  50.6 us (7%)
  starting transfers between devices  44.3 us (6%)
    psum x3, blocking collectives, norm_total(): return lax.psum(jnp.sum(vector * vector), 'sec')  224 us
    all_to_all x2, waiting for transfers between devices, per_device(): lax.all_to_all(jnp.stack([moving] * lax.axis_size('sec')), 'sec', 0, 0)  158 us
    psum x2, blocking collectives, per_device(): rayleigh = lax.psum(jnp.sum(vector * image_vec), 'sec')  142 us
    dot_general x24, matrix products, product(): return jnp.matmul(left, right, precision=HIGH)  52.4 us
    ppermute x14, starting transfers between devices, passed_along(): lax.ppermute(value, axis, [(source, source + steps) for source in range(i...  32.9 us
    ppermute x14, waiting for transfers between devices, passed_along(): lax.ppermute(value, axis, [(source, source + steps) for source in range(i...  25.6 us
    dot_general x2, matrix products, per_device(): jnp.einsum('ji,ipc->jpc', chooser, shard_piece, precision=HIGH)  22.2 us
    unnamed x15, local copies, waits for them, and re-layouts  18.1 us
  transfers between devices with their start and end apart: 16, of which 8 were waited for; matrix products, arithmetic and copies ran while one was open for 13% of the time, Pallas kernels for 0%

profile of v1, /device:TPU:8, one launch (start us, length us, event | category | flops | bytes accessed | tf_op | source)
XLA Modules:
  0.0 739.9 jit_solution(1678159028273070738)
XLA Ops:
  4.3 78.3 %psum.35 = f32[]{:T(128)} all-reduce(f32[]{:T(128)} %fusion.65), channel_id=1, replica_groups=mesh['seg'=8,'sec'=32] {'sec'}, use_global_device_ids=true, to_apply=%region_1.2 | all-reduce | flops 1 | bytes 8 | tf_op jit(solution)/shard_map/psum | solution.py:26
  84.8 4.1 stack.6
  88.9 5.1 all-to-all-start
  96.3 5.8 collective-permute-done
  104.4 5.8 collective-permute-done.1
  112.5 5.8 collective-permute-done.2
  154.4 18.1 %copy.26 = f32[1,1,18,256,256]{2,4,3,1,0:T(8,128)} copy(f32[1,1,18,256,256]{4,3,2,1,0:T(8,128)} %param.11) | data formatting | bytes 9437184 | tf_op args[2]
  177.5 6.1 fusion.12
  187.6 10.2 %fusion.18 = f32[18,256,256]{2,0,1:T(8,128)} fusion(f32[18,256,256]{2,1,0:T(8,128)S(1)} %fusion.10, f32[18,18]{1,0:T(8,128)S(1)} %collective-permute-done.13, pred[]{:T(512)S(6)} %eq.81), kind=kOutput, calls=%fused_computation.20 | convolution fusion | flops 254804944 | bytes 9438481 | tf_op jit(solution)/shard_map/vw,bvij->bwij/dot_general | solution.py:65
  197.8 17.6 %copy.29 = f32[18,256,256]{0,2,1:T(8,128)} copy(f32[18,256,256]{2,0,1:T(8,128)} %fusion.18) | data formatting | bytes 9437184 | tf_op jit(solution)/shard_map/squeeze | solution.py:18
  217.8 7.8 %fusion.16 = f32[18,256,256]{2,1,0:T(8,128)S(1)} fusion(f32[18,256,256]{2,0,1:T(8,128)} %fusion.18, f32[1,1,256,256]{3,2,1,0:T(8,128)S(1)} %copy-done.2, f32[]{:T(128)S(6)} %sqrt.9, f32[256]{0:T(256)S(1)} %get-tuple-element.16, f32[256]{0:T(256)S(1)} %get-tuple-element.17), kind=kOutput, calls=%fused_computation.18 | convolution fusion | flops 3624075264 | bytes 9701380 | tf_op jit(solution)/shard_map/dot_general | solution.py:18
  225.6 9.7 %fusion.28 = f32[256,256]{1,0:T(8,128)S(1)} fusion(f32[18,256,256]{2,1,0:T(8,128)S(1)} %fusion.16, f32[1,1,18,256,256]{4,3,2,1,0:T(8,128)} %param.11), kind=kOutput, calls=%fused_computation.35 | convolution fusion | flops 3623878656 | bytes 9699328 | tf_op jit(solution)/shard_map/dot_general | solution.py:18
  235.3 32.0 %all-to-all-done = f32[32,1,256,256]{3,2,1,0:T(8,128)} async-done(((f32[32,1,256,256]{3,2,1,0:T(8,128)}), f32[32,1,256,256]{3,2,1,0:T(8,128)}, u32[]{:S(2)}, u32[]{:S(2)}) %all-to-all-start) | async-done | bytes 8388640 | tf_op jit(solution)/shard_map/all_to_all | solution.py:84
  267.3 11.1 %fusion.2 = f32[1,256,256]{2,0,1:T(1,128)S(1)} fusion(f32[32,256,256]{2,1,0:T(8,128)} %bitcast.38, s32[]{:T(128)} %bitcast.34), kind=kOutput, calls=%fused_computation.4 | convolution fusion | flops 25165856 | bytes 8650756 | tf_op jit(solution)/shard_map/ji,ipc->jpc/dot_general | solution.py:88
  279.5 70.7 %psum.36 = f32[]{:T(128)} all-reduce(f32[]{:T(128)} %get-tuple-element.11), channel_id=1, replica_groups=mesh['seg'=8,'sec'=32] {'sec'}, use_global_device_ids=true, to_apply=%region_3.4 | all-reduce | flops 1 | bytes 8 | tf_op jit(solution)/shard_map/psum | solution.py:92
  352.0 74.7 %psum.37 = f32[]{:T(128)} all-reduce(f32[]{:T(128)} %get-tuple-element.7), channel_id=1, replica_groups=mesh['seg'=8,'sec'=32] {'sec'}, use_global_device_ids=true, to_apply=%region_5.6 | all-reduce | flops 1 | bytes 8 | tf_op jit(solution)/shard_map/psum | solution.py:26
  427.8 4.2 stack.7
  431.9 6.4 all-to-all-start.1
  438.3 7.5 %fusion.14 = f32[18,256,256]{2,1,0:T(8,128)S(1)} fusion(f32[18,256,256]{2,0,1:T(8,128)} %fusion.18, f32[256,256]{1,0:T(8,128)S(1)} %get-tuple-element.8, f32[]{:T(128)S(6)} %sqrt.10), kind=kOutput, calls=%fused_computation.16 | convolution fusion | flops 3623944192 | bytes 9699332 | tf_op jit(solution)/shard_map/dot_general | solution.py:18
  445.8 9.8 %fusion.25 = f32[256,256]{1,0:T(8,128)S(1)} fusion(f32[18,256,256]{2,1,0:T(8,128)S(1)} %fusion.14, f32[1,1,18,256,256]{4,3,2,1,0:T(8,128)} %param.11), kind=kOutput, calls=%fused_computation.34 | convolution fusion | flops 3623878656 | bytes 9699328 | tf_op jit(solution)/shard_map/dot_general | solution.py:18
  455.6 126.5 %all-to-all-done.1 = f32[32,1,256,256]{3,2,1,0:T(8,128)} async-done(((f32[32,1,256,256]{3,2,1,0:T(8,128)}), f32[32,1,256,256]{3,2,1,0:T(8,128)}, u32[]{:S(2)}, u32[]{:S(2)}) %all-to-all-start.1) | async-done | bytes 8388640 | tf_op jit(solution)/shard_map/all_to_all | solution.py:84
  582.1 11.1 %fusion = f32[1,256,256]{2,0,1:T(1,128)S(1)} fusion(f32[32,256,256]{2,1,0:T(8,128)} %bitcast.49, s32[]{:T(128)} %bitcast.34), kind=kOutput, calls=%fused_computation.2 | convolution fusion | flops 25165856 | bytes 8650756 | tf_op jit(solution)/shard_map/ji,ipc->jpc/dot_general | solution.py:88
  594.2 71.6 %psum.38 = f32[]{:T(128)} all-reduce(f32[]{:T(128)} %get-tuple-element.14), channel_id=1, replica_groups=mesh['seg'=8,'sec'=32] {'sec'}, use_global_device_ids=true, to_apply=%region_7.8 | all-reduce | flops 1 | bytes 8 | tf_op jit(solution)/shard_map/psum | solution.py:92
  667.1 70.8 %psum.39 = f32[]{:T(128)} all-reduce(f32[]{:T(128)} %get-tuple-element.5), channel_id=1, replica_groups=mesh['seg'=8,'sec'=32] {'sec'}, use_global_device_ids=true, to_apply=%region_9.10 | all-reduce | flops 1 | bytes 8 | tf_op jit(solution)/shard_map/psum | solution.py:26
  (69 shorter events, 66.2 us)
Async XLA Ops:
  0.0 94.0 %copy-start = (f32[1,1,256,256]{3,2,1,0:T(8,128)S(1)}, f32[1,1,256,256]{3,2,1,0:T(8,128)}, u32[]{:S(2)}) copy-start(f32[1,1,256,256]{3,2,1,0:T(8,128)} %param.12) | copy-start | bytes 786436
  88.9 31.6 %copy-start.3 = (f32[1,18,18]{2,0,1:T(1,128)S(1)}, f32[1,18,18]{2,0,1:T(1,128)}, u32[]{:S(2)}) copy-start(f32[1,18,18]{2,0,1:T(1,128)} %param.13) | copy-start | bytes 3892
  88.9 178.4 %all-to-all-start = ((f32[32,1,256,256]{3,2,1,0:T(8,128)}), f32[32,1,256,256]{3,2,1,0:T(8,128)}, u32[]{:S(2)}, u32[]{:S(2)}) async-start(f32[32,1,256,256]{3,2,1,0:T(8,128)} %stack.6), calls=%async_computation | async-start | bytes 16777216 | tf_op jit(solution)/shard_map/all_to_all | solution.py:84
  94.0 59.8 %copy-start.6 = (s32[1,32]{1,0:T(1,128)S(1)}, s32[1,32]{1,0:T(1,128)}, u32[]{:S(2)}) copy-start(s32[1,32]{1,0:T(1,128)} %param.17) | copy-start | bytes 388
  94.3 7.7 %collective-permute-start = (f32[1,256,256]{2,1,0:T(8,128)S(1)}, f32[1,256,256]{2,1,0:T(8,128)S(1)}, u32[]{:S(2)}, u32[]{:S(2)}) collective-permute-start(f32[1,256,256]{2,1,0:T(8,128)S(1)} %convolution_bitcast_fusion.8), channel_id=1, source_target_pairs={{0,32},{32,64},{64,96},{96,128},{128,160},{160,192},{192,224},{1,3... | collective-permute-start | bytes 786440 | tf_op jit(solution)/shard_map/ppermute | solution.py:14
  102.4 7.7 %collective-permute-start.1 = (f32[1,256,256]{2,1,0:T(8,128)S(1)}, f32[1,256,256]{2,1,0:T(8,128)S(1)}, u32[]{:S(2)}, u32[]{:S(2)}) collective-permute-start(f32[1,256,256]{2,1,0:T(8,128)S(1)} %convolution_bitcast_fusion.7), channel_id=1, source_target_pairs={{0,32},{32,64},{64,96},{96,128},{128,160},{160,192},{192,224},{1,3... | collective-permute-start | bytes 786440 | tf_op jit(solution)/shard_map/ppermute | solution.py:14
  110.5 7.7 %collective-permute-start.2 = (f32[1,256,256]{2,1,0:T(8,128)S(1)}, f32[1,256,256]{2,1,0:T(8,128)S(1)}, u32[]{:S(2)}, u32[]{:S(2)}) collective-permute-start(f32[1,256,256]{2,1,0:T(8,128)S(1)} %convolution_bitcast_fusion.6), channel_id=1, source_target_pairs={{0,32},{32,64},{64,96},{96,128},{128,160},{160,192},{192,224},{1,3... | collective-permute-start | bytes 786440 | tf_op jit(solution)/shard_map/ppermute | solution.py:14
  118.6 9.9 %collective-permute-start.3 = (f32[1,256,256]{2,1,0:T(8,128)S(1)}, f32[1,256,256]{2,1,0:T(8,128)S(1)}, u32[]{:S(2)}, u32[]{:S(2)}) collective-permute-start(f32[1,256,256]{2,1,0:T(8,128)S(1)} %convolution_bitcast_fusion.5), channel_id=1, source_target_pairs={{0,32},{32,64},{64,96},{96,128},{128,160},{160,192},{192,224},{1,3... | collective-permute-start | bytes 786440 | tf_op jit(solution)/shard_map/ppermute | solution.py:14
  120.7 5.8 collective-permute-start.7
  126.6 5.9 collective-permute-start.8
  128.9 10.8 %collective-permute-start.4 = (f32[1,256,256]{2,1,0:T(8,128)S(1)}, f32[1,256,256]{2,1,0:T(8,128)S(1)}, u32[]{:S(2)}, u32[]{:S(2)}) collective-permute-start(f32[1,256,256]{2,1,0:T(8,128)S(1)} %convolution_bitcast_fusion.4), channel_id=1, source_target_pairs={{0,32},{32,64},{64,96},{96,128},{128,160},{160,192},{192,224},{1,3... | collective-permute-start | bytes 786440 | tf_op jit(solution)/shard_map/ppermute | solution.py:14
  132.7 5.0 collective-permute-start.9
  137.8 5.6 collective-permute-start.10
  140.2 10.6 %collective-permute-start.5 = (f32[1,256,256]{2,1,0:T(8,128)S(1)}, f32[1,256,256]{2,1,0:T(8,128)S(1)}, u32[]{:S(2)}, u32[]{:S(2)}) collective-permute-start(f32[1,256,256]{2,1,0:T(8,128)S(1)} %convolution_bitcast_fusion.3), channel_id=1, source_target_pairs={{0,32},{32,64},{64,96},{96,128},{128,160},{160,192},{192,224},{1,3... | collective-permute-start | bytes 786440 | tf_op jit(solution)/shard_map/ppermute | solution.py:14
  143.6 5.0 collective-permute-start.11
  148.8 26.0 %collective-permute-start.12 = (f32[18,18]{1,0:T(8,128)S(1)}, f32[18,18]{1,0:T(8,128)S(1)}, u32[]{:S(2)}, u32[]{:S(2)}) collective-permute-start(f32[18,18]{1,0:T(8,128)S(1)} %fusion.80), channel_id=1, source_target_pairs={{0,32},{32,64},{64,96},{96,128},{128,160},{160,192},{192,224},{1,3... | collective-permute-start | bytes 3896 | tf_op jit(solution)/shard_map/ppermute | solution.py:14
  151.1 26.3 %collective-permute-start.6 = (f32[1,256,256]{2,1,0:T(8,128)S(1)}, f32[1,256,256]{2,1,0:T(8,128)S(1)}, u32[]{:S(2)}, u32[]{:S(2)}) collective-permute-start(f32[1,256,256]{2,1,0:T(8,128)S(1)} %convolution_bitcast_fusion.2), channel_id=1, source_target_pairs={{0,32},{32,64},{64,96},{96,128},{128,160},{160,192},{192,224},{1,3... | collective-permute-start | bytes 786440 | tf_op jit(solution)/shard_map/ppermute | solution.py:14
  175.0 12.6 %collective-permute-start.13 = (f32[18,18]{1,0:T(8,128)S(1)}, f32[18,18]{1,0:T(8,128)S(1)}, u32[]{:S(2)}, u32[]{:S(2)}) collective-permute-start(f32[18,18]{1,0:T(8,128)S(1)} %fusion.81), channel_id=1, source_target_pairs={{0,32},{32,64},{64,96},{96,128},{128,160},{160,192},{192,224},{1,3... | collective-permute-start | bytes 3896 | tf_op jit(solution)/shard_map/ppermute | solution.py:14
  197.8 20.0 %copy-start.2 = (f32[1,1,256,256]{3,2,1,0:T(8,128)S(1)}, f32[1,1,256,256]{3,2,1,0:T(8,128)}, u32[]{:S(2)}) copy-start(f32[1,1,256,256]{3,2,1,0:T(8,128)} %param.9) | copy-start | bytes 786436
  235.3 43.1 %copy-start.5 = (f32[1,1,256,256]{3,2,1,0:T(8,128)S(1)}, f32[1,1,256,256]{3,2,1,0:T(8,128)}, u32[]{:S(2)}) copy-start(f32[1,1,256,256]{3,2,1,0:T(8,128)} %param.14) | copy-start | bytes 786436
  267.3 160.1 %copy-start.4 = (f32[1,1,256,256]{3,2,1,0:T(8,128)S(1)}, f32[1,1,256,256]{3,2,1,0:T(8,128)}, u32[]{:S(2)}) copy-start(f32[1,1,256,256]{3,2,1,0:T(8,128)} %param.15) | copy-start | bytes 786436
  431.9 150.1 %all-to-all-start.1 = ((f32[32,1,256,256]{3,2,1,0:T(8,128)}), f32[32,1,256,256]{3,2,1,0:T(8,128)}, u32[]{:S(2)}, u32[]{:S(2)}) async-start(f32[32,1,256,256]{3,2,1,0:T(8,128)} %stack.7), calls=%async_computation.1 | async-start | bytes 16777216 | tf_op jit(solution)/shard_map/all_to_all | solution.py:84
  582.1 157.3 %copy-start.1 = (f32[1,1,256,256]{3,2,1,0:T(8,128)S(1)}, f32[1,1,256,256]{3,2,1,0:T(8,128)}, u32[]{:S(2)}) copy-start(f32[1,1,256,256]{3,2,1,0:T(8,128)} %param.12) | copy-start | bytes 786436
